TPU v7x, 32 devices: a whole 2x2x4 slice. The times are simulated.
32 devices in a mesh: ctx: 8 (over y, x, core), uly: 4 (over z).
Axes of the slice: x: 2, y: 2, z: 4, core: 2. Of those that a mesh axis runs over, the one named last changes fastest.
Arguments:
- query_states: bfloat16 [1024, 2048], P(('ctx', 'uly')), may hold values from -8 to 8
- key_states: bfloat16 [1024, 2048], P(('ctx', 'uly')), may hold values from -8 to 8
- value_states: bfloat16 [1024, 2048], P(('ctx', 'uly')), may hold values from -6 to 6
- score_kernel: float32 [16, 6, 11], P('uly'), may hold values from -0.4 to 1.2
- head_mixing: float32 [16, 4], P('uly'), may hold values from 0.25 to 1
- head_gain: float32 [2048], P('uly'), may hold values from 0.5 to 1.5
Outputs:
- attended: bfloat16 [1024, 2048], P(('ctx', 'uly'))
All inputs are finite; a program needn't handle non-finite values.
Results may differ from a plain program's by a relative error of at most 0.0049.
Values may be sent and summed in bfloat16 or wider, within the bound.
No kernel may reach another device: no remote copies, remote signals or barrier semaphores. Data moves between devices by JAX's collectives and lax.ppermute only.
A program may use at most 64 MiB of HBM per device.

v0:
```python
import jax
import jax.numpy as jnp
from jax import lax
from jax.sharding import PartitionSpec as P

GROUP = 4
QCONV = 6
KCONV = 11
lowest = -1e30
epsilon = 1e-06


def passed_along(shard, axis, by):
    peers = lax.axis_size(axis)
    pairs = [(i, i + by) for i in range(peers) if 0 <= i + by < peers]
    return lax.ppermute(shard, axis, pairs)


def partner_2(shard, axis, bit):
    return lax.ppermute(shard, axis, [(i, i ^ 1 << bit) for i in range(lax.axis_size(axis))])


def unchanged(carried):
    return carried


def group_span(shard_count, shard_rows):
    span_size = 1
    while span_size * 2 * shard_rows <= 512 and shard_count % (span_size * 2) == 0:
        span_size = span_size * 2
    return span_size


def tile_logits(query_rows, query_first, key_rows, key_first, score_kernel):
    row_lead = QCONV - 1
    col_lead = KCONV - 1
    heads = score_kernel.shape[0]
    row_count = query_rows.shape[0] - row_lead
    span_size = key_rows.shape[0]
    padded_cols = key_rows.shape[1]
    col_count = padded_cols - col_lead
    query_heads = query_rows.reshape(query_rows.shape[0], heads, -1)
    key_heads = key_rows.reshape(span_size, padded_cols, heads, -1)
    dot_scores = jnp.einsum(
        "qhd,nkhd->nhqk", query_heads, key_heads, preferred_element_type=jnp.float32
    )
    dot_scores = dot_scores * query_heads.shape[2] ** (-0.5)
    query_pos = query_first - row_lead + lax.iota(jnp.int32, query_rows.shape[0])
    key_pos = (
        key_first
        - col_lead
        + col_count * lax.iota(jnp.int32, span_size)[:, None]
        + lax.iota(jnp.int32, padded_cols)[None, :]
    )
    inside = (
        (key_pos[:, None, :] <= query_pos[None, :, None])
        & (key_pos[:, None, :] >= 0)
        & (query_pos[None, :, None] >= 0)
    )
    dot_scores = jnp.where(inside[:, None], dot_scores, 0.0)
    convolved = jnp.zeros((span_size, heads, row_count, col_count), jnp.float32)
    for row_lag in range(QCONV):
        for col_lag in range(KCONV):
            window = dot_scores[
                :,
                :,
                row_lead - row_lag : row_lead - row_lag + row_count,
                col_lead - col_lag : col_lead - col_lag + col_count,
            ]
            convolved = convolved + score_kernel[None, :, row_lag, col_lag, None, None] * window
    causal = key_pos[:, None, col_lead:] <= query_pos[None, row_lead:, None]
    return jnp.where(causal[:, None], convolved, lowest)


def stats_block(query_block, key_rows, key_first, stats_pair, score_kernel):
    query_rows, query_first = query_block
    last_query = query_first + query_rows.shape[0] - QCONV

    def stats_compute(current):
        logits = tile_logits(query_rows, query_first, key_rows, key_first, score_kernel)
        running_max, running_sum = current
        fresh_max = jnp.maximum(running_max, jnp.max(logits, axis=(0, 3)))
        rescaled = running_sum * jnp.exp(running_max - fresh_max)
        return (
            fresh_max,
            rescaled + jnp.sum(jnp.exp(logits - fresh_max[None, :, :, None]), axis=(0, 3)),
        )

    return lax.cond(key_first <= last_query, stats_compute, unchanged, stats_pair)


def output_block(
    query_block, key_rows, value_rows, key_first, weighted, stats_pair, score_kernel, head_mixing
):
    query_rows, query_first = query_block
    last_query = query_first + query_rows.shape[0] - QCONV

    def output_compute(current):
        logits = tile_logits(query_rows, query_first, key_rows, key_first, score_kernel)
        running_max, running_sum = stats_pair
        probabilities = (
            jnp.exp(logits - running_max[None, :, :, None]) / running_sum[None, :, :, None]
        )
        span_size, heads, row_count, col_count = probabilities.shape
        grouped = probabilities.reshape(span_size, heads // GROUP, GROUP, row_count, col_count)
        weights = head_mixing.reshape(heads // GROUP, GROUP, GROUP)
        mixed_probs = jnp.zeros_like(grouped)
        for source in range(GROUP):
            mixed_probs = (
                mixed_probs + weights[None, :, :, source, None, None] * grouped[:, :, source, None]
            )
        mixed_probs = mixed_probs.reshape(probabilities.shape).astype(jnp.bfloat16)
        value_heads = value_rows.reshape(span_size, col_count, heads, -1)
        return current + jnp.einsum(
            "nhqk,nkhd->qhd", mixed_probs, value_heads, preferred_element_type=jnp.float32
        )

    return lax.cond(key_first <= last_query, output_compute, unchanged, weighted)


def stats_sweep(query_blocks, key_stack, stats_all, score_kernel):
    shard_rows = key_stack.shape[1] - (KCONV - 1)
    span_size = group_span(key_stack.shape[0], shard_rows)
    spans = key_stack.reshape((key_stack.shape[0] // span_size, span_size) + key_stack.shape[1:])

    def stats_advance(step_index, carried):
        key_rows = lax.dynamic_index_in_dim(spans, step_index, 0, keepdims=False)
        key_first = step_index * span_size * shard_rows
        return tuple(
            (
                stats_block(query_block, key_rows, key_first, stats_pair, score_kernel)
                for query_block, stats_pair in zip(query_blocks, carried)
            )
        )

    return lax.fori_loop(0, spans.shape[0], stats_advance, stats_all)


def output_sweep(
    query_blocks, key_stack, value_stack, weighted_all, stats_all, score_kernel, head_mixing
):
    shard_rows = value_stack.shape[1]
    span_size = group_span(key_stack.shape[0], shard_rows)
    key_spans = key_stack.reshape(
        (key_stack.shape[0] // span_size, span_size) + key_stack.shape[1:]
    )
    value_spans = value_stack.reshape(
        (value_stack.shape[0] // span_size, span_size) + value_stack.shape[1:]
    )

    def output_advance(step_index, carried):
        key_rows = lax.dynamic_index_in_dim(key_spans, step_index, 0, keepdims=False)
        value_rows = lax.dynamic_index_in_dim(value_spans, step_index, 0, keepdims=False)
        key_first = step_index * span_size * shard_rows
        return tuple(
            (
                output_block(
                    query_block,
                    key_rows,
                    value_rows,
                    key_first,
                    weighted,
                    stats_pair,
                    score_kernel,
                    head_mixing,
                )
                for query_block, weighted, stats_pair in zip(query_blocks, carried, stats_all)
            )
        )

    return lax.fori_loop(0, key_spans.shape[0], output_advance, weighted_all)


def normalize(weighted, gain_local):
    factor = lax.rsqrt(jnp.mean(weighted * weighted, axis=2, keepdims=True) + epsilon)
    return (
        (weighted * factor * gain_local[None]).astype(jnp.bfloat16).reshape(weighted.shape[0], -1)
    )


def shards(query_states, key_states, value_states, score_kernel, head_mixing, head_gain):
    query_local, key_local, value_local = (
        lax.all_to_all(query_states, "uly", split_axis=1, concat_axis=0, tiled=True),
        lax.all_to_all(key_states, "uly", split_axis=1, concat_axis=0, tiled=True),
        lax.all_to_all(value_states, "uly", split_axis=1, concat_axis=0, tiled=True),
    )
    shard_rows = query_local.shape[0]
    row_lead = QCONV - 1
    col_lead = KCONV - 1
    heads = score_kernel.shape[0]
    head_dim = query_local.shape[1] // heads
    ctx_count = lax.axis_size("ctx")
    ctx_place = lax.axis_index("ctx")
    tails = jnp.concatenate(
        [query_local[shard_rows - row_lead :], key_local[shard_rows - col_lead :]], axis=0
    )
    earlier = passed_along(tails, "ctx", 1)
    query_ext = jnp.concatenate([earlier[:row_lead], query_local], axis=0)
    key_ext = jnp.concatenate([earlier[row_lead:], key_local], axis=0)
    query_first = ctx_place * shard_rows
    half_rows = shard_rows // 2
    top_bit = ctx_count.bit_length() - 2
    far_rows = partner_2(query_ext[half_rows:], "ctx", top_bit)
    partner = jnp.where(
        ctx_place < ctx_count // 2, ctx_place + ctx_count // 2, ctx_place - ctx_count // 2
    )
    query_blocks = [
        (query_ext[: half_rows + row_lead], query_first),
        (far_rows, partner * shard_rows + half_rows),
    ]
    stats_all = tuple(
        (
            (
                jnp.full((heads, block_rows.shape[0] - row_lead), lowest, jnp.float32),
                jnp.zeros((heads, block_rows.shape[0] - row_lead), jnp.float32),
            )
            for block_rows, block_first in query_blocks
        )
    )
    weighted_all = tuple(
        (
            jnp.zeros((block_rows.shape[0] - row_lead, heads, head_dim), jnp.float32)
            for block_rows, block_first in query_blocks
        )
    )
    key_stack = key_ext[None]
    value_stack = value_local[None]
    stats_all = stats_sweep(
        query_blocks, lax.all_gather(key_stack, "ctx", axis=0, tiled=True), stats_all, score_kernel
    )
    weighted_all = output_sweep(
        query_blocks,
        lax.all_gather(key_stack, "ctx", axis=0, tiled=True),
        lax.all_gather(value_stack, "ctx", axis=0, tiled=True),
        weighted_all,
        stats_all,
        score_kernel,
        head_mixing,
    )
    gain_local = head_gain.reshape(heads, head_dim)
    finished = [normalize(weighted, gain_local) for weighted in weighted_all]
    returned = partner_2(finished[1], "ctx", top_bit)
    attended = jnp.concatenate([finished[0], returned], axis=0)
    return lax.all_to_all(attended, "uly", split_axis=0, concat_axis=1, tiled=True)


def solution(mesh):
    placed = (
        P(("ctx", "uly"), None),
        P(("ctx", "uly"), None),
        P(("ctx", "uly"), None),
        P("uly", None, None),
        P("uly", None),
        P("uly"),
    )
    return jax.shard_map(
        shards, mesh=mesh, in_specs=placed, out_specs=P(("ctx", "uly"), None), check_vma=False
    )
```

profile of v0, /device:TPU:0, one launch (start us, length us, event | category | flops | bytes accessed | tf_op | source)
XLA Modules:
  0.0 152.9 jit_solution(973212687336004941)
XLA Ops:
  6.5 1.6 %copy.144 = bf16[4,4,8,512]{3,2,0,1:T(8,128)(2,1)} copy(bf16[4,4,8,512]{3,2,1,0:T(8,128)(2,1)} %bitcast.667) | data formatting | bytes 262144 | tf_op jit(solution)/shard_map/all_to_all | solution.py:184
  8.1 6.4 %all-to-all-start.1 = ((bf16[32,4,512]{2,0,1:T(8,128)(2,1)}), bf16[32,4,512]{2,0,1:T(8,128)(2,1)S(1)}, u32[]{:S(2)}, u32[]{:S(2)}) async-start(bf16[32,4,512]{2,0,1:T(8,128)(2,1)} %bitcast.640), calls=%async_computation.1 | async-start | bytes 262144 | tf_op jit(solution)/shard_map/all_to_all | solution.py:184
  14.6 1.6 %copy.145 = bf16[4,4,8,512]{3,2,0,1:T(8,128)(2,1)} copy(bf16[4,4,8,512]{3,2,1,0:T(8,128)(2,1)} %bitcast.668) | data formatting | bytes 262144 | tf_op jit(solution)/shard_map/all_to_all | solution.py:183
  16.2 4.5 %all-to-all-done.1 = bf16[32,4,512]{2,0,1:T(8,128)(2,1)S(1)} async-done(((bf16[32,4,512]{2,0,1:T(8,128)(2,1)}), bf16[32,4,512]{2,0,1:T(8,128)(2,1)S(1)}, u32[]{:S(2)}, u32[]{:S(2)}) %all-to-all-start.1) | async-done | bytes 131104 | tf_op jit(solution)/shard_map/all_to_all | solution.py:184
  20.7 3.3 %all-to-all-start = ((bf16[32,4,512]{2,0,1:T(8,128)(2,1)}), bf16[32,4,512]{2,0,1:T(8,128)(2,1)S(1)}, u32[]{:S(2)}, u32[]{:S(2)}) async-start(bf16[32,4,512]{2,0,1:T(8,128)(2,1)} %bitcast.641), calls=%async_computation | async-start | bytes 262144 | tf_op jit(solution)/shard_map/all_to_all | solution.py:183
  24.1 5.8 %all-to-all-done = bf16[32,4,512]{2,0,1:T(8,128)(2,1)S(1)} async-done(((bf16[32,4,512]{2,0,1:T(8,128)(2,1)}), bf16[32,4,512]{2,0,1:T(8,128)(2,1)S(1)}, u32[]{:S(2)}, u32[]{:S(2)}) %all-to-all-start) | async-done | bytes 131104 | tf_op jit(solution)/shard_map/all_to_all | solution.py:183
  29.9 1.3 collective-permute-start
  32.8 9.0 %all_to_all.73 = bf16[32,4,512]{2,0,1:T(8,128)(2,1)} all-to-all(bf16[32,4,512]{2,0,1:T(8,128)(2,1)S(1)} %bitcast.665), channel_id=1, replica_groups=mesh['ctx'=8,'uly'=4] {'uly'}, dimensions={1} | all-to-all | bytes 262144 | tf_op jit(solution)/shard_map/all_to_all | solution.py:185
  41.9 5.4 %collective-permute-start.1 = (bf16[69,512]{1,0:T(8,128)(2,1)S(1)}, bf16[69,512]{1,0:T(8,128)(2,1)S(1)}, u32[]{:S(2)}, u32[]{:S(2)}) collective-permute-start(bf16[69,512]{1,0:T(8,128)(2,1)S(1)} %get-tuple-element.1401), channel_id=1, source_target_pairs={{0,16},{4,20},{8,24},{12,28},{16,0},{20,4},{24,8},{28,12},{1,17},{... | collective-permute-start | bytes 211976 | tf_op jit(solution)/shard_map/ppermute | solution.py:20
  47.4 2.2 %collective-permute-done.1 = bf16[69,512]{1,0:T(8,128)(2,1)S(1)} collective-permute-done((bf16[69,512]{1,0:T(8,128)(2,1)S(1)}, bf16[69,512]{1,0:T(8,128)(2,1)S(1)}, u32[]{:S(2)}, u32[]{:S(2)}) %collective-permute-start.1) | collective-permute-done | bytes 70688 | tf_op jit(solution)/shard_map/ppermute | solution.py:20
  49.6 9.5 %all-gather.7.cloned.1.call-done = bf16[8,138,512]{2,1,0:T(8,128)(2,1)} async-done(((bf16[1,138,512]{2,1,0:T(8,128)(2,1)}), bf16[8,138,512]{2,1,0:T(8,128)(2,1)}) %all-gather.7.cloned.1.call-update) | async-done | bytes 1130512 | tf_op jit(solution)/shard_map/all_gather | solution.py:233
  59.1 34.9 %while.46 = (s32[]{:T(128)}, f32[4,64]{1,0:T(4,128)S(1)}, f32[4,64]{1,0:T(4,128)S(1)}, f32[4,64]{1,0:T(4,128)S(1)}, f32[4,64]{1,0:T(4,128)S(1)}, /*index=5*/s32[...) while((s32[]{:T(128)}, f32[4,64]{1,0:T(4,128)S(1)}, ...), condition=%wide.region_9.10_spmd, body=%wide.region_0.9_spmd.sunk | while | flops 114301904 | bytes 77811088 | solution.py:136
  59.1 1.1 dynamic-slice_bitcast_fusion.6
  60.2 10.9 %conditional.8 = ((f32[4,64]{1,0:T(4,128)S(1)}, f32[4,64]{1,0:T(4,128)S(1)})) conditional(s32[]{:T(128)} %convert_element_type.72, (f32[4,64]{1,0:T(4,128)S(1)}, f32[4,64]{1,0:T(4,128)S(1)}) %tuple.395, (s32[]{:T(128)}, s32[]{:T(128)}, f32[4,6,11]{0,2,1:T(8,128)S(1)}, bf16[4,138,512]{2,1,0:T(8,128)(2,1)S(1)}, bf16[69,512]{1,0:T(8,128)(2,1)S(1)}, ...), branch_computations={%region_1.1_spmd, %region_2.4_spmd} | conditional | flops 57150952 | bytes 38340128 | solution.py:89
  61.7 9.2 %fusion.312 = (f32[4,64]{1,0:T(4,128)S(1)}, f32[4,4,64,128]{3,2,0,1:T(8,128)S(1)}) fusion(f32[4,4,69,138]{3,2,0,1:T(8,128)S(1)} %fusion.1, f32[4]{0:T(128)S(1)} %get-tuple-element.1270, f32[4]{0:T(128)S(1)} %get-tuple-element.1271, f32[4]{0:T(128)S(1)} %get-tuple-element.1272, f32[4]{0:T(128)S(1)} %get-tuple-element.1273, f32[4]{0:T(128)S(1)} %get-tuple-element.1274, ...), kind=kLoop, calls=%fused_computation.914 | loop fusion | flops 17432320 | bytes 35162144 | tf_op jit(solution)/shard_map/while/body/eval_jaxpr/cond/branch_1_fun/reduce_max | solution.py:82
  71.1 10.9 %conditional.9 = ((f32[4,64]{1,0:T(4,128)S(1)}, f32[4,64]{1,0:T(4,128)S(1)})) conditional(s32[]{:T(128)} %convert_element_type.73, (f32[4,64]{1,0:T(4,128)S(1)}, f32[4,64]{1,0:T(4,128)S(1)}) %tuple.397, (s32[]{:T(128)}, s32[]{:T(128)}, f32[4,6,11]{0,2,1:T(8,128)S(1)}, bf16[4,138,512]{2,1,0:T(8,128)(2,1)S(1)}, bf16[69,512]{1,0:T(8,128)(2,1)S(1)}, ...), branch_computations={%region_5.5_spmd, %region_6.8_spmd} | conditional | flops 57150952 | bytes 38340128 | solution.py:89
  72.5 9.2 %fusion.314 = (f32[4,64]{1,0:T(4,128)S(1)}, f32[4,4,64,128]{3,2,0,1:T(8,128)S(1)}) fusion(f32[4,4,69,138]{3,2,0,1:T(8,128)S(1)} %fusion.71, f32[4]{0:T(128)S(1)} %get-tuple-element.1336, f32[4]{0:T(128)S(1)} %get-tuple-element.1337, f32[4]{0:T(128)S(1)} %get-tuple-element.1338, f32[4]{0:T(128)S(1)} %get-tuple-element.1339, f32[4]{0:T(128)S(1)} %get-tuple-element.1340, ...), kind=kLoop, calls=%fused_computation.915 | loop fusion | flops 17432320 | bytes 35162144 | tf_op jit(solution)/shard_map/while/body/eval_jaxpr/cond/branch_1_fun/reduce_max | solution.py:82
  82.0 1.1 dynamic-slice_bitcast_fusion.6
  83.2 10.9 %conditional.9 = ((f32[4,64]{1,0:T(4,128)S(1)}, f32[4,64]{1,0:T(4,128)S(1)})) conditional(s32[]{:T(128)} %convert_element_type.73, (f32[4,64]{1,0:T(4,128)S(1)}, f32[4,64]{1,0:T(4,128)S(1)}) %tuple.397, (s32[]{:T(128)}, s32[]{:T(128)}, f32[4,6,11]{0,2,1:T(8,128)S(1)}, bf16[4,138,512]{2,1,0:T(8,128)(2,1)S(1)}, bf16[69,512]{1,0:T(8,128)(2,1)S(1)}, ...), branch_computations={%region_5.5_spmd, %region_6.8_spmd} | conditional | flops 57150952 | bytes 38340128 | solution.py:89
  84.6 9.2 %fusion.314 = (f32[4,64]{1,0:T(4,128)S(1)}, f32[4,4,64,128]{3,2,0,1:T(8,128)S(1)}) fusion(f32[4,4,69,138]{3,2,0,1:T(8,128)S(1)} %fusion.71, f32[4]{0:T(128)S(1)} %get-tuple-element.1336, f32[4]{0:T(128)S(1)} %get-tuple-element.1337, f32[4]{0:T(128)S(1)} %get-tuple-element.1338, f32[4]{0:T(128)S(1)} %get-tuple-element.1339, f32[4]{0:T(128)S(1)} %get-tuple-element.1340, ...), kind=kLoop, calls=%fused_computation.915 | loop fusion | flops 17432320 | bytes 35162144 | tf_op jit(solution)/shard_map/while/body/eval_jaxpr/cond/branch_1_fun/reduce_max | solution.py:82
  94.1 36.3 %while.47 = (s32[]{:T(128)}, f32[64,4,128]{2,0,1:T(8,128)S(1)}, f32[64,4,128]{2,0,1:T(8,128)S(1)}, s32[]{:T(128)}, bf16[2,4,138,512]{3,2,1,0:T(8,128)(2,1)}, /*i...) while((s32[]{:T(128)}, f32[64,4,128]{2,0,1:T(8,128)S(1)}, ...), condition=%wide.region_15.16_spmd, body=%wide.region_10.15_spmd.sunk | while | flops 183310304 | bytes 86701888 | solution.py:171
  94.3 1.2 dynamic-slice_bitcast_fusion.7
  95.8 11.1 %conditional.10 = (f32[64,4,128]{2,0,1:T(8,128)S(1)}) conditional(s32[]{:T(128)} %convert_element_type.74, f32[64,4,128]{2,0,1:T(8,128)S(1)} %get-tuple-element.1670, (f32[4,4]{1,0:T(4,128)S(1)}, s32[]{:T(128)}, s32[]{:T(128)}, f32[4,6,11]{0,2,1:T(8,128)S(1)}, bf16[4,138,512]{2,1,0:T(8,128)(2,1)S(1)}, /*index=5*/bf16[69,512]{1,0:T(8,128)(2,1)S(1)}, ...), branch_computations={%region_11.11_spmd, %region_12.12_spmd} | conditional | flops 91655144 | bytes 40164048 | solution.py:118
  97.2 9.0 %fusion.151 = f32[4,1,4,64,128]{4,3,0,2,1:T(8,128)S(1)} fusion(f32[4,4,69,138]{3,2,0,1:T(8,128)S(1)} %fusion.141, f32[4,64]{1,0:T(4,128)S(1)} %get-tuple-element.865, f32[4,64]{1,0:T(4,128)S(1)} %get-tuple-element.864, f32[4]{0:T(128)S(1)} %get-tuple-element.1134, f32[4]{0:T(128)S(1)} %get-tuple-element.1135, f32[4]{0:T(128)S(1)} %get-tuple-element.1136, ...), kind=kLoop, calls=%fused_computation.439 | loop fusion | flops 17563648 | bytes 35163168 | tf_op jit(solution)/shard_map/while/body/eval_jaxpr/cond/branch_1_fun/reshape | solution.py:105
  106.8 11.0 %conditional.11 = (f32[64,4,128]{2,0,1:T(8,128)S(1)}) conditional(s32[]{:T(128)} %convert_element_type.75, f32[64,4,128]{2,0,1:T(8,128)S(1)} %get-tuple-element.1671, (f32[4,4]{1,0:T(4,128)S(1)}, s32[]{:T(128)}, s32[]{:T(128)}, f32[4,6,11]{0,2,1:T(8,128)S(1)}, bf16[4,138,512]{2,1,0:T(8,128)(2,1)S(1)}, /*index=5*/bf16[69,512]{1,0:T(8,128)(2,1)S(1)}, ...), branch_computations={%region_13.13_spmd, %region_14.14_spmd} | conditional | flops 91655144 | bytes 40164048 | solution.py:118
  108.2 9.0 %fusion.236 = f32[4,1,4,64,128]{4,3,0,2,1:T(8,128)S(1)} fusion(f32[4,4,69,138]{3,2,0,1:T(8,128)S(1)} %fusion.226, f32[4,64]{1,0:T(4,128)S(1)} %get-tuple-element.875, f32[4,64]{1,0:T(4,128)S(1)} %get-tuple-element.874, f32[4]{0:T(128)S(1)} %get-tuple-element.1204, f32[4]{0:T(128)S(1)} %get-tuple-element.1205, f32[4]{0:T(128)S(1)} %get-tuple-element.1206, ...), kind=kLoop, calls=%fused_computation.674 | loop fusion | flops 17563648 | bytes 35163168 | tf_op jit(solution)/shard_map/while/body/eval_jaxpr/cond/branch_1_fun/reshape | solution.py:105
  117.9 1.2 dynamic-slice_bitcast_fusion.7
  119.4 11.0 %conditional.11 = (f32[64,4,128]{2,0,1:T(8,128)S(1)}) conditional(s32[]{:T(128)} %convert_element_type.75, f32[64,4,128]{2,0,1:T(8,128)S(1)} %get-tuple-element.1671, (f32[4,4]{1,0:T(4,128)S(1)}, s32[]{:T(128)}, s32[]{:T(128)}, f32[4,6,11]{0,2,1:T(8,128)S(1)}, bf16[4,138,512]{2,1,0:T(8,128)(2,1)S(1)}, /*index=5*/bf16[69,512]{1,0:T(8,128)(2,1)S(1)}, ...), branch_computations={%region_13.13_spmd, %region_14.14_spmd} | conditional | flops 91655144 | bytes 40164048 | solution.py:118
  120.8 9.0 %fusion.236 = f32[4,1,4,64,128]{4,3,0,2,1:T(8,128)S(1)} fusion(f32[4,4,69,138]{3,2,0,1:T(8,128)S(1)} %fusion.226, f32[4,64]{1,0:T(4,128)S(1)} %get-tuple-element.875, f32[4,64]{1,0:T(4,128)S(1)} %get-tuple-element.874, f32[4]{0:T(128)S(1)} %get-tuple-element.1204, f32[4]{0:T(128)S(1)} %get-tuple-element.1205, f32[4]{0:T(128)S(1)} %get-tuple-element.1206, ...), kind=kLoop, calls=%fused_computation.674 | loop fusion | flops 17563648 | bytes 35163168 | tf_op jit(solution)/shard_map/while/body/eval_jaxpr/cond/branch_1_fun/reshape | solution.py:105
  130.8 1.5 collective-permute-start.2
  132.3 2.8 %collective-permute-done.2 = bf16[64,512]{1,0:T(8,128)(2,1)S(1)} collective-permute-done((bf16[64,512]{1,0:T(8,128)(2,1)S(1)}, bf16[64,512]{1,0:T(8,128)(2,1)S(1)}, u32[]{:S(2)}, u32[]{:S(2)}) %collective-permute-start.2) | collective-permute-done | bytes 65568 | tf_op jit(solution)/shard_map/ppermute | solution.py:20
  135.1 10.3 %all_to_all.74 = bf16[4,32,512]{2,1,0:T(8,128)(2,1)S(1)} all-to-all(bf16[4,32,512]{2,1,0:T(8,128)(2,1)S(1)} %bitcast.663), channel_id=1, replica_groups=mesh['ctx'=8,'uly'=4] {'uly'}, dimensions={0} | all-to-all | bytes 262144 | tf_op jit(solution)/shard_map/all_to_all | solution.py:244
  (162 shorter events, 13.9 us)
Async XLA Ops:
  6.5 26.3 %copy-start.2 = (bf16[32,2048]{1,0:T(8,128)(2,1)S(1)}, bf16[32,2048]{1,0:T(8,128)(2,1)}, u32[]{:S(2)}) copy-start(bf16[32,2048]{1,0:T(8,128)(2,1)} %param.20) | copy-start | bytes 393220
  8.1 39.2 %copy-start.3 = (f32[4,6,11]{2,0,1:T(4,128)S(1)}, f32[4,6,11]{2,0,1:T(4,128)}, u32[]{:S(2)}) copy-start(f32[4,6,11]{2,0,1:T(4,128)} %param.21) | copy-start | bytes 3172
  8.1 12.5 %all-to-all-start.1 = ((bf16[32,4,512]{2,0,1:T(8,128)(2,1)}), bf16[32,4,512]{2,0,1:T(8,128)(2,1)S(1)}, u32[]{:S(2)}, u32[]{:S(2)}) async-start(bf16[32,4,512]{2,0,1:T(8,128)(2,1)} %bitcast.640), calls=%async_computation.1 | async-start | bytes 262144 | tf_op jit(solution)/shard_map/all_to_all | solution.py:184
  20.7 9.2 %all-to-all-start = ((bf16[32,4,512]{2,0,1:T(8,128)(2,1)}), bf16[32,4,512]{2,0,1:T(8,128)(2,1)S(1)}, u32[]{:S(2)}, u32[]{:S(2)}) async-start(bf16[32,4,512]{2,0,1:T(8,128)(2,1)} %bitcast.641), calls=%async_computation | async-start | bytes 262144 | tf_op jit(solution)/shard_map/all_to_all | solution.py:183
  24.0 35.1 %all-gather.7.cloned.1.call-start = ((), (), s32[]{:S(2)}) async-start(), calls=%async_computation.5 | async-start | bytes 1327104 | tf_op jit(solution)/shard_map/all_gather | solution.py:233
  29.9 2.1 %collective-permute-start = (bf16[15,512]{1,0:T(8,128)(2,1)S(1)}, bf16[15,512]{1,0:T(8,128)(2,1)S(1)}, u32[]{:S(2)}, u32[]{:S(2)}) collective-permute-start(bf16[15,512]{1,0:T(8,128)(2,1)S(1)} %pad_maximum_fusion.2), channel_id=1, source_target_pairs={{0,4},{4,8},{8,12},{12,16},{16,20},{20,24},{24,28},{1,5},{5,9},{9,... | collective-permute-start | bytes 46088 | tf_op jit(solution)/shard_map/ppermute | solution.py:16
  32.8 61.3 %all-gather.5.cloned.1.call-start = ((), (), s32[]{:S(2)}) async-start(), calls=%async_computation.4 | async-start | bytes 1179648 | tf_op jit(solution)/shard_map/all_gather | solution.py:234
  41.9 7.7 %collective-permute-start.1 = (bf16[69,512]{1,0:T(8,128)(2,1)S(1)}, bf16[69,512]{1,0:T(8,128)(2,1)S(1)}, u32[]{:S(2)}, u32[]{:S(2)}) collective-permute-start(bf16[69,512]{1,0:T(8,128)(2,1)S(1)} %get-tuple-element.1401), channel_id=1, source_target_pairs={{0,16},{4,20},{8,24},{12,28},{16,0},{20,4},{24,8},{28,12},{1,17},{... | collective-permute-start | bytes 211976 | tf_op jit(solution)/shard_map/ppermute | solution.py:20
  59.1 35.0 %copy-start.1 = (f32[4,4]{1,0:T(4,128)S(1)}, f32[4,4]{1,0:T(4,128)}, u32[]{:S(2)}) copy-start(f32[4,4]{1,0:T(4,128)} %param.22) | copy-start | bytes 196
  94.1 36.5 %copy-start.4 = (f32[512]{0:T(512)S(1)}, f32[512]{0:T(512)}, u32[]{:S(2)}) copy-start(f32[512]{0:T(512)} %param.23) | copy-start | bytes 6148
  94.3 1.4 copy-start
  117.9 1.4 copy-start
  130.8 4.3 %collective-permute-start.2 = (bf16[64,512]{1,0:T(8,128)(2,1)S(1)}, bf16[64,512]{1,0:T(8,128)(2,1)S(1)}, u32[]{:S(2)}, u32[]{:S(2)}) collective-permute-start(bf16[64,512]{1,0:T(8,128)(2,1)S(1)} %bitcast.670), channel_id=1, source_target_pairs={{0,16},{4,20},{8,24},{12,28},{16,0},{20,4},{24,8},{28,12},{1,17},{... | collective-permute-start | bytes 196616 | tf_op jit(solution)/shard_map/ppermute | solution.py:20
Sparse Core Ops, SparseCore 0:
  32.9 26.1 all-gather.6
  61.0 23.6 all-gather.4
where the time goes:
time: 154 us; the launch traced here: 153 us
  other arithmetic  58.6 us (38%)
  waiting for transfers between devices  25.7 us (17%)
  blocking collectives  19.3 us (13%)
  starting transfers between devices  18 us (12%)
  between operations  13.6 us (9%)
  local copies, waits for them, and re-layouts  12.4 us (8%)
  matrix products  4.27 us (3%)
    reduce_max x3, other arithmetic, stats_compute(): fresh_max = jnp.maximum(running_max, jnp.max(logits, axis=(0, 3)))  27.5 us
    reshape x3, other arithmetic, output_compute(): probabilities.reshape(span_size, heads // GROUP, GROUP, row_count, col_co...  27 us
    all_to_all x1, blocking collectives, shards(): lax.all_to_all(attended, 'uly', split_axis=0, concat_axis=1, tiled=True)  10.3 us
    all_gather x1, waiting for transfers between devices, shards(): lax.all_gather(key_stack, 'ctx', axis=0, tiled=True)  9.46 us
    all_to_all x1, blocking collectives, shards(): lax.all_to_all(value_states, 'uly', split_axis=1, concat_axis=0, tiled=True)  9.01 us
    ppermute x2, starting transfers between devices, partner_2(): lax.ppermute(shard, axis, [(i, i ^ 1 << bit) for i in range(lax.axis_size...  6.88 us
    all_to_all x1, starting transfers between devices, shards(): lax.all_to_all(key_states, 'uly', split_axis=1, concat_axis=0, tiled=True)  6.45 us
    all_to_all x1, waiting for transfers between devices, shards(): lax.all_to_all(query_states, 'uly', split_axis=1, concat_axis=0, tiled=True)  5.82 us
  transfers between devices with their start and end apart: 7, of which 6 were waited for; matrix products, arithmetic and copies ran while one was open for 24% of the time, Pallas kernels for 0%

commit v1 on v0

--- a/solution.py
+++ b/solution.py
@@ -181,7 +181,12 @@
 def shards(query_states, key_states, value_states, score_kernel, head_mixing, head_gain):
     query_local, key_local, value_local = (
         lax.all_to_all(query_states, "uly", split_axis=1, concat_axis=0, tiled=True),
-        lax.all_to_all(key_states, "uly", split_axis=1, concat_axis=0, tiled=True),
+        jnp.concatenate(
+            lax.all_to_all(
+                jnp.stack(jnp.split(key_states, lax.axis_size("uly"), axis=1), axis=0), "uly", 0, 0
+            ),
+            axis=0,
+        ),
         lax.all_to_all(value_states, "uly", split_axis=1, concat_axis=0, tiled=True),
     )
     shard_rows = query_local.shape[0]

time: 154 us -> 153 us (level)
    all_to_all x1 -> x0, local copies, waits for them, and re-layouts: 1.6 us -> none  [shards(): lax.all_to_all(key_states, 'uly', split_axis=1, concat_axis=0, tiled=True)]
where the time goes in v1:
time: 153 us
  other arithmetic  59.3 us (39%)
  waiting for transfers between devices  25.7 us (17%)
  blocking collectives  19.3 us (13%)
  starting transfers between devices  18 us (12%)
  between operations  13.6 us (9%)
  local copies, waits for them, and re-layouts  11.6 us (8%)
  matrix products  4.26 us (3%)
    reduce_max x3, other arithmetic, stats_compute(): fresh_max = jnp.maximum(running_max, jnp.max(logits, axis=(0, 3)))  27.5 us
    reshape x3, other arithmetic, output_compute(): probabilities.reshape(span_size, heads // GROUP, GROUP, row_count, col_co...  27 us
    all_to_all x1, blocking collectives, shards(): lax.all_to_all(attended, 'uly', split_axis=0, concat_axis=1, tiled=True)  10.3 us
    all_gather x1, waiting for transfers between devices, shards(): lax.all_gather(key_stack, 'ctx', axis=0, tiled=True)  9.46 us
    all_to_all x1, blocking collectives, shards(): lax.all_to_all(value_states, 'uly', split_axis=1, concat_axis=0, tiled=True)  9 us
    ppermute x2, starting transfers between devices, partner_2(): lax.ppermute(shard, axis, [(i, i ^ 1 << bit) for i in range(lax.axis_size...  6.88 us
    all_to_all x1, starting transfers between devices, shards(): lax.all_to_all(jnp.stack(jnp.split(key_states, lax.axis_size('uly'), axis...  6.45 us
    all_to_all x1, waiting for transfers between devices, shards(): lax.all_to_all(query_states, 'uly', split_axis=1, concat_axis=0, tiled=True)  5.82 us
  transfers between devices with their start and end apart: 7, of which 6 were waited for; matrix products, arithmetic and copies ran while one was open for 24% of the time, Pallas kernels for 0%

profile of v1, /device:TPU:0, one launch (start us, length us, event | category | flops | bytes accessed | tf_op | source)
XLA Modules:
  0.0 152.9 jit_solution(4188716929185169899)
XLA Ops:
  6.5 0.9 slice_bitcast_fusion.275
  8.1 6.4 %all-to-all-start.1 = ((bf16[4,32,512]{2,1,0:T(8,128)(2,1)}), bf16[4,32,512]{2,1,0:T(8,128)(2,1)S(1)}, u32[]{:S(2)}, u32[]{:S(2)}) async-start(bf16[4,32,512]{2,1,0:T(8,128)(2,1)} %pad_maximum_fusion), calls=%async_computation.1 | async-start | bytes 262144 | tf_op jit(solution)/shard_map/all_to_all | solution.py:185
  14.5 1.6 %copy.137 = bf16[4,4,8,512]{3,2,0,1:T(8,128)(2,1)} copy(bf16[4,4,8,512]{3,2,1,0:T(8,128)(2,1)} %bitcast.669) | data formatting | bytes 262144 | tf_op jit(solution)/shard_map/all_to_all | solution.py:183
  16.1 4.5 %all-to-all-done.1 = bf16[4,32,512]{2,1,0:T(8,128)(2,1)S(1)} async-done(((bf16[4,32,512]{2,1,0:T(8,128)(2,1)}), bf16[4,32,512]{2,1,0:T(8,128)(2,1)S(1)}, u32[]{:S(2)}, u32[]{:S(2)}) %all-to-all-start.1) | async-done | bytes 131104 | tf_op jit(solution)/shard_map/all_to_all | solution.py:185
  20.6 3.3 %all-to-all-start = ((bf16[32,4,512]{2,0,1:T(8,128)(2,1)}), bf16[32,4,512]{2,0,1:T(8,128)(2,1)S(1)}, u32[]{:S(2)}, u32[]{:S(2)}) async-start(bf16[32,4,512]{2,0,1:T(8,128)(2,1)} %bitcast.643), calls=%async_computation | async-start | bytes 262144 | tf_op jit(solution)/shard_map/all_to_all | solution.py:183
  24.0 5.8 %all-to-all-done = bf16[32,4,512]{2,0,1:T(8,128)(2,1)S(1)} async-done(((bf16[32,4,512]{2,0,1:T(8,128)(2,1)}), bf16[32,4,512]{2,0,1:T(8,128)(2,1)S(1)}, u32[]{:S(2)}, u32[]{:S(2)}) %all-to-all-start) | async-done | bytes 131104 | tf_op jit(solution)/shard_map/all_to_all | solution.py:183
  29.8 1.3 collective-permute-start
  32.8 9.0 %all_to_all.59 = bf16[32,4,512]{2,0,1:T(8,128)(2,1)} all-to-all(bf16[32,4,512]{2,0,1:T(8,128)(2,1)S(1)} %bitcast.667), channel_id=1, replica_groups=mesh['ctx'=8,'uly'=4] {'uly'}, dimensions={1} | all-to-all | bytes 262144 | tf_op jit(solution)/shard_map/all_to_all | solution.py:190
  41.8 5.4 %collective-permute-start.1 = (bf16[69,512]{1,0:T(8,128)(2,1)S(1)}, bf16[69,512]{1,0:T(8,128)(2,1)S(1)}, u32[]{:S(2)}, u32[]{:S(2)}) collective-permute-start(bf16[69,512]{1,0:T(8,128)(2,1)S(1)} %get-tuple-element.1401), channel_id=1, source_target_pairs={{0,16},{4,20},{8,24},{12,28},{16,0},{20,4},{24,8},{28,12},{1,17},{... | collective-permute-start | bytes 211976 | tf_op jit(solution)/shard_map/ppermute | solution.py:20
  47.3 2.2 %collective-permute-done.1 = bf16[69,512]{1,0:T(8,128)(2,1)S(1)} collective-permute-done((bf16[69,512]{1,0:T(8,128)(2,1)S(1)}, bf16[69,512]{1,0:T(8,128)(2,1)S(1)}, u32[]{:S(2)}, u32[]{:S(2)}) %collective-permute-start.1) | collective-permute-done | bytes 70688 | tf_op jit(solution)/shard_map/ppermute | solution.py:20
  49.6 9.5 %all-gather.7.cloned.1.call-done = bf16[8,138,512]{2,1,0:T(8,128)(2,1)} async-done(((bf16[1,138,512]{2,1,0:T(8,128)(2,1)}), bf16[8,138,512]{2,1,0:T(8,128)(2,1)}) %all-gather.7.cloned.1.call-update) | async-done | bytes 1130512 | tf_op jit(solution)/shard_map/all_gather | solution.py:238
  59.0 34.9 %while.46 = (s32[]{:T(128)}, f32[4,64]{1,0:T(4,128)S(1)}, f32[4,64]{1,0:T(4,128)S(1)}, f32[4,64]{1,0:T(4,128)S(1)}, f32[4,64]{1,0:T(4,128)S(1)}, /*index=5*/s32[...) while((s32[]{:T(128)}, f32[4,64]{1,0:T(4,128)S(1)}, ...), condition=%wide.region_9.10_spmd, body=%wide.region_0.9_spmd.sunk | while | flops 114301904 | bytes 77811088 | solution.py:136
  59.1 1.1 dynamic-slice_bitcast_fusion.6
  60.2 10.9 %conditional.8 = ((f32[4,64]{1,0:T(4,128)S(1)}, f32[4,64]{1,0:T(4,128)S(1)})) conditional(s32[]{:T(128)} %convert_element_type.72, (f32[4,64]{1,0:T(4,128)S(1)}, f32[4,64]{1,0:T(4,128)S(1)}) %tuple.398, (s32[]{:T(128)}, s32[]{:T(128)}, f32[4,6,11]{0,2,1:T(8,128)S(1)}, bf16[4,138,512]{2,1,0:T(8,128)(2,1)S(1)}, bf16[69,512]{1,0:T(8,128)(2,1)S(1)}, ...), branch_computations={%region_1.1_spmd, %region_2.4_spmd} | conditional | flops 57150952 | bytes 38340128 | solution.py:89
  61.6 9.2 %fusion.312 = (f32[4,64]{1,0:T(4,128)S(1)}, f32[4,4,64,128]{3,2,0,1:T(8,128)S(1)}) fusion(f32[4,4,69,138]{3,2,0,1:T(8,128)S(1)} %fusion.1, f32[4]{0:T(128)S(1)} %get-tuple-element.1270, f32[4]{0:T(128)S(1)} %get-tuple-element.1271, f32[4]{0:T(128)S(1)} %get-tuple-element.1272, f32[4]{0:T(128)S(1)} %get-tuple-element.1273, f32[4]{0:T(128)S(1)} %get-tuple-element.1274, ...), kind=kLoop, calls=%fused_computation.918 | loop fusion | flops 17432320 | bytes 35162144 | tf_op jit(solution)/shard_map/while/body/eval_jaxpr/cond/branch_1_fun/reduce_max | solution.py:82
  71.0 10.9 %conditional.9 = ((f32[4,64]{1,0:T(4,128)S(1)}, f32[4,64]{1,0:T(4,128)S(1)})) conditional(s32[]{:T(128)} %convert_element_type.73, (f32[4,64]{1,0:T(4,128)S(1)}, f32[4,64]{1,0:T(4,128)S(1)}) %tuple.400, (s32[]{:T(128)}, s32[]{:T(128)}, f32[4,6,11]{0,2,1:T(8,128)S(1)}, bf16[4,138,512]{2,1,0:T(8,128)(2,1)S(1)}, bf16[69,512]{1,0:T(8,128)(2,1)S(1)}, ...), branch_computations={%region_5.5_spmd, %region_6.8_spmd} | conditional | flops 57150952 | bytes 38340128 | solution.py:89
  72.5 9.2 %fusion.314 = (f32[4,64]{1,0:T(4,128)S(1)}, f32[4,4,64,128]{3,2,0,1:T(8,128)S(1)}) fusion(f32[4,4,69,138]{3,2,0,1:T(8,128)S(1)} %fusion.71, f32[4]{0:T(128)S(1)} %get-tuple-element.1336, f32[4]{0:T(128)S(1)} %get-tuple-element.1337, f32[4]{0:T(128)S(1)} %get-tuple-element.1338, f32[4]{0:T(128)S(1)} %get-tuple-element.1339, f32[4]{0:T(128)S(1)} %get-tuple-element.1340, ...), kind=kLoop, calls=%fused_computation.919 | loop fusion | flops 17432320 | bytes 35162144 | tf_op jit(solution)/shard_map/while/body/eval_jaxpr/cond/branch_1_fun/reduce_max | solution.py:82
  81.9 1.1 dynamic-slice_bitcast_fusion.6
  83.1 10.9 %conditional.9 = ((f32[4,64]{1,0:T(4,128)S(1)}, f32[4,64]{1,0:T(4,128)S(1)})) conditional(s32[]{:T(128)} %convert_element_type.73, (f32[4,64]{1,0:T(4,128)S(1)}, f32[4,64]{1,0:T(4,128)S(1)}) %tuple.400, (s32[]{:T(128)}, s32[]{:T(128)}, f32[4,6,11]{0,2,1:T(8,128)S(1)}, bf16[4,138,512]{2,1,0:T(8,128)(2,1)S(1)}, bf16[69,512]{1,0:T(8,128)(2,1)S(1)}, ...), branch_computations={%region_5.5_spmd, %region_6.8_spmd} | conditional | flops 57150952 | bytes 38340128 | solution.py:89
  84.5 9.2 %fusion.314 = (f32[4,64]{1,0:T(4,128)S(1)}, f32[4,4,64,128]{3,2,0,1:T(8,128)S(1)}) fusion(f32[4,4,69,138]{3,2,0,1:T(8,128)S(1)} %fusion.71, f32[4]{0:T(128)S(1)} %get-tuple-element.1336, f32[4]{0:T(128)S(1)} %get-tuple-element.1337, f32[4]{0:T(128)S(1)} %get-tuple-element.1338, f32[4]{0:T(128)S(1)} %get-tuple-element.1339, f32[4]{0:T(128)S(1)} %get-tuple-element.1340, ...), kind=kLoop, calls=%fused_computation.919 | loop fusion | flops 17432320 | bytes 35162144 | tf_op jit(solution)/shard_map/while/body/eval_jaxpr/cond/branch_1_fun/reduce_max | solution.py:82
  94.0 36.3 %while.47 = (s32[]{:T(128)}, f32[64,4,128]{2,0,1:T(8,128)S(1)}, f32[64,4,128]{2,0,1:T(8,128)S(1)}, s32[]{:T(128)}, bf16[2,4,138,512]{3,2,1,0:T(8,128)(2,1)}, /*i...) while((s32[]{:T(128)}, f32[64,4,128]{2,0,1:T(8,128)S(1)}, ...), condition=%wide.region_15.16_spmd, body=%wide.region_10.15_spmd.sunk | while | flops 183310304 | bytes 86701888 | solution.py:171
  94.2 1.2 dynamic-slice_bitcast_fusion.7
  95.7 11.1 %conditional.10 = (f32[64,4,128]{2,0,1:T(8,128)S(1)}) conditional(s32[]{:T(128)} %convert_element_type.74, f32[64,4,128]{2,0,1:T(8,128)S(1)} %get-tuple-element.1674, (f32[4,4]{1,0:T(4,128)S(1)}, s32[]{:T(128)}, s32[]{:T(128)}, f32[4,6,11]{0,2,1:T(8,128)S(1)}, bf16[4,138,512]{2,1,0:T(8,128)(2,1)S(1)}, /*index=5*/bf16[69,512]{1,0:T(8,128)(2,1)S(1)}, ...), branch_computations={%region_11.11_spmd, %region_12.12_spmd} | conditional | flops 91655144 | bytes 40164048 | solution.py:118
  97.1 9.0 %fusion.151 = f32[4,1,4,64,128]{4,3,0,2,1:T(8,128)S(1)} fusion(f32[4,4,69,138]{3,2,0,1:T(8,128)S(1)} %fusion.141, f32[4,64]{1,0:T(4,128)S(1)} %get-tuple-element.865, f32[4,64]{1,0:T(4,128)S(1)} %get-tuple-element.864, f32[4]{0:T(128)S(1)} %get-tuple-element.1134, f32[4]{0:T(128)S(1)} %get-tuple-element.1135, f32[4]{0:T(128)S(1)} %get-tuple-element.1136, ...), kind=kLoop, calls=%fused_computation.439 | loop fusion | flops 17563648 | bytes 35163168 | tf_op jit(solution)/shard_map/while/body/eval_jaxpr/cond/branch_1_fun/reshape | solution.py:105
  106.7 11.0 %conditional.11 = (f32[64,4,128]{2,0,1:T(8,128)S(1)}) conditional(s32[]{:T(128)} %convert_element_type.75, f32[64,4,128]{2,0,1:T(8,128)S(1)} %get-tuple-element.1675, (f32[4,4]{1,0:T(4,128)S(1)}, s32[]{:T(128)}, s32[]{:T(128)}, f32[4,6,11]{0,2,1:T(8,128)S(1)}, bf16[4,138,512]{2,1,0:T(8,128)(2,1)S(1)}, /*index=5*/bf16[69,512]{1,0:T(8,128)(2,1)S(1)}, ...), branch_computations={%region_13.13_spmd, %region_14.14_spmd} | conditional | flops 91655144 | bytes 40164048 | solution.py:118
  108.1 9.0 %fusion.236 = f32[4,1,4,64,128]{4,3,0,2,1:T(8,128)S(1)} fusion(f32[4,4,69,138]{3,2,0,1:T(8,128)S(1)} %fusion.226, f32[4,64]{1,0:T(4,128)S(1)} %get-tuple-element.875, f32[4,64]{1,0:T(4,128)S(1)} %get-tuple-element.874, f32[4]{0:T(128)S(1)} %get-tuple-element.1204, f32[4]{0:T(128)S(1)} %get-tuple-element.1205, f32[4]{0:T(128)S(1)} %get-tuple-element.1206, ...), kind=kLoop, calls=%fused_computation.674 | loop fusion | flops 17563648 | bytes 35163168 | tf_op jit(solution)/shard_map/while/body/eval_jaxpr/cond/branch_1_fun/reshape | solution.py:105
  117.8 1.2 dynamic-slice_bitcast_fusion.7
  119.3 11.0 %conditional.11 = (f32[64,4,128]{2,0,1:T(8,128)S(1)}) conditional(s32[]{:T(128)} %convert_element_type.75, f32[64,4,128]{2,0,1:T(8,128)S(1)} %get-tuple-element.1675, (f32[4,4]{1,0:T(4,128)S(1)}, s32[]{:T(128)}, s32[]{:T(128)}, f32[4,6,11]{0,2,1:T(8,128)S(1)}, bf16[4,138,512]{2,1,0:T(8,128)(2,1)S(1)}, /*index=5*/bf16[69,512]{1,0:T(8,128)(2,1)S(1)}, ...), branch_computations={%region_13.13_spmd, %region_14.14_spmd} | conditional | flops 91655144 | bytes 40164048 | solution.py:118
  120.7 9.0 %fusion.236 = f32[4,1,4,64,128]{4,3,0,2,1:T(8,128)S(1)} fusion(f32[4,4,69,138]{3,2,0,1:T(8,128)S(1)} %fusion.226, f32[4,64]{1,0:T(4,128)S(1)} %get-tuple-element.875, f32[4,64]{1,0:T(4,128)S(1)} %get-tuple-element.874, f32[4]{0:T(128)S(1)} %get-tuple-element.1204, f32[4]{0:T(128)S(1)} %get-tuple-element.1205, f32[4]{0:T(128)S(1)} %get-tuple-element.1206, ...), kind=kLoop, calls=%fused_computation.674 | loop fusion | flops 17563648 | bytes 35163168 | tf_op jit(solution)/shard_map/while/body/eval_jaxpr/cond/branch_1_fun/reshape | solution.py:105
  130.7 1.5 collective-permute-start.2
  132.2 2.8 %collective-permute-done.2 = bf16[64,512]{1,0:T(8,128)(2,1)S(1)} collective-permute-done((bf16[64,512]{1,0:T(8,128)(2,1)S(1)}, bf16[64,512]{1,0:T(8,128)(2,1)S(1)}, u32[]{:S(2)}, u32[]{:S(2)}) %collective-permute-start.2) | collective-permute-done | bytes 65568 | tf_op jit(solution)/shard_map/ppermute | solution.py:20
  135.0 10.3 %all_to_all.60 = bf16[4,32,512]{2,1,0:T(8,128)(2,1)S(1)} all-to-all(bf16[4,32,512]{2,1,0:T(8,128)(2,1)S(1)} %bitcast.665), channel_id=1, replica_groups=mesh['ctx'=8,'uly'=4] {'uly'}, dimensions={0} | all-to-all | bytes 262144 | tf_op jit(solution)/shard_map/all_to_all | solution.py:249
  (163 shorter events, 14.6 us)
Async XLA Ops:
  6.5 26.2 %copy-start.2 = (bf16[32,2048]{1,0:T(8,128)(2,1)S(1)}, bf16[32,2048]{1,0:T(8,128)(2,1)}, u32[]{:S(2)}) copy-start(bf16[32,2048]{1,0:T(8,128)(2,1)} %param.20) | copy-start | bytes 393220
  8.1 39.2 %copy-start.3 = (f32[4,6,11]{2,0,1:T(4,128)S(1)}, f32[4,6,11]{2,0,1:T(4,128)}, u32[]{:S(2)}) copy-start(f32[4,6,11]{2,0,1:T(4,128)} %param.21) | copy-start | bytes 3172
  8.1 12.5 %all-to-all-start.1 = ((bf16[4,32,512]{2,1,0:T(8,128)(2,1)}), bf16[4,32,512]{2,1,0:T(8,128)(2,1)S(1)}, u32[]{:S(2)}, u32[]{:S(2)}) async-start(bf16[4,32,512]{2,1,0:T(8,128)(2,1)} %pad_maximum_fusion), calls=%async_computation.1 | async-start | bytes 262144 | tf_op jit(solution)/shard_map/all_to_all | solution.py:185
  20.6 9.2 %all-to-all-start = ((bf16[32,4,512]{2,0,1:T(8,128)(2,1)}), bf16[32,4,512]{2,0,1:T(8,128)(2,1)S(1)}, u32[]{:S(2)}, u32[]{:S(2)}) async-start(bf16[32,4,512]{2,0,1:T(8,128)(2,1)} %bitcast.643), calls=%async_computation | async-start | bytes 262144 | tf_op jit(solution)/shard_map/all_to_all | solution.py:183
  23.9 35.1 %all-gather.7.cloned.1.call-start = ((), (), s32[]{:S(2)}) async-start(), calls=%async_computation.5 | async-start | bytes 1327104 | tf_op jit(solution)/shard_map/all_gather | solution.py:238
  29.8 2.1 %collective-permute-start = (bf16[15,512]{1,0:T(8,128)(2,1)S(1)}, bf16[15,512]{1,0:T(8,128)(2,1)S(1)}, u32[]{:S(2)}, u32[]{:S(2)}) collective-permute-start(bf16[15,512]{1,0:T(8,128)(2,1)S(1)} %pad_maximum_fusion.3), channel_id=1, source_target_pairs={{0,4},{4,8},{8,12},{12,16},{16,20},{20,24},{24,28},{1,5},{5,9},{9,... | collective-permute-start | bytes 46088 | tf_op jit(solution)/shard_map/ppermute | solution.py:16
  32.7 61.3 %all-gather.5.cloned.1.call-start = ((), (), s32[]{:S(2)}) async-start(), calls=%async_computation.4 | async-start | bytes 1179648 | tf_op jit(solution)/shard_map/all_gather | solution.py:239
  41.8 7.7 %collective-permute-start.1 = (bf16[69,512]{1,0:T(8,128)(2,1)S(1)}, bf16[69,512]{1,0:T(8,128)(2,1)S(1)}, u32[]{:S(2)}, u32[]{:S(2)}) collective-permute-start(bf16[69,512]{1,0:T(8,128)(2,1)S(1)} %get-tuple-element.1401), channel_id=1, source_target_pairs={{0,16},{4,20},{8,24},{12,28},{16,0},{20,4},{24,8},{28,12},{1,17},{... | collective-permute-start | bytes 211976 | tf_op jit(solution)/shard_map/ppermute | solution.py:20
  59.0 35.0 %copy-start.1 = (f32[4,4]{1,0:T(4,128)S(1)}, f32[4,4]{1,0:T(4,128)}, u32[]{:S(2)}) copy-start(f32[4,4]{1,0:T(4,128)} %param.22) | copy-start | bytes 196
  94.0 36.5 %copy-start.4 = (f32[512]{0:T(512)S(1)}, f32[512]{0:T(512)}, u32[]{:S(2)}) copy-start(f32[512]{0:T(512)} %param.23) | copy-start | bytes 6148
  94.2 1.4 copy-start
  117.8 1.4 copy-start
  130.7 4.3 %collective-permute-start.2 = (bf16[64,512]{1,0:T(8,128)(2,1)S(1)}, bf16[64,512]{1,0:T(8,128)(2,1)S(1)}, u32[]{:S(2)}, u32[]{:S(2)}) collective-permute-start(bf16[64,512]{1,0:T(8,128)(2,1)S(1)} %bitcast.671), channel_id=1, source_target_pairs={{0,16},{4,20},{8,24},{12,28},{16,0},{20,4},{24,8},{28,12},{1,17},{... | collective-permute-start | bytes 196616 | tf_op jit(solution)/shard_map/ppermute | solution.py:20
Sparse Core Ops, SparseCore 0:
  32.8 26.1 all-gather.6
  60.9 23.6 all-gather.4
